TPU v7x, 32 devices: a whole 2x2x4 slice. The times are simulated.
32 devices in a mesh: groups: 2 (over y), slide: 4 (over z), rep: 2 (over x), section: 2 (over core).
Axes of the slice: x: 2, y: 2, z: 4, core: 2. Of those that a mesh axis runs over, the one named last changes fastest.
Arguments:
- tile_features: bfloat16 [8, 12, 49, 1536], P(('groups', 'rep', 'section'), 'slide'), parts along dimension 0, may hold values from -6 to 6
- depth_weight: float32 [49, 1536], replicated, may hold values from -0.875 to 0.875
- depth_bias: float32 [1536], replicated, may hold values from -3 to 3
- norm_gain: float32 [1536], replicated, may hold values from 0.1 to 1.9
- norm_bias: float32 [1536], replicated, may hold values from -3 to 3
- up_weight: bfloat16 [1536, 3072], P(None, 'rep'), may hold values from -0.15625 to 0.15625
- up_bias: float32 [3072], P('rep'), may hold values from -3 to 3
- down_weight: bfloat16 [3072, 1536], P('rep'), may hold values from -0.109375 to 0.109375
- down_bias: float32 [1536], replicated, may hold values from -3 to 3
- layer_scale: float32 [1536], replicated, may hold values from 0.3 to 3
- head_gain: float32 [1536], replicated, may hold values from 0.1 to 1.9
- head_bias: float32 [1536], replicated, may hold values from -3 to 3
- embed_store: bfloat16 [8, 512, 1536], P(('groups', 'rep', 'section'), 'slide'), parts along dimension 0, may hold values from -6 to 6
- in_weight: bfloat16 [1536, 1024], P('slide'), may hold values from -0.15625 to 0.15625
- slide_gain: float32 [1024], replicated, may hold values from 0.1 to 1.9
- qkv_weight: bfloat16 [1024, 3072], P(None, 'slide'), may hold values from -0.1875 to 0.1875
- head_slopes: float32 [16], replicated, may hold values from 0.004 to 0.4
- tile_coords: int32 [8, 2, 512], P(('groups', 'rep', 'section')), parts along dimension 0, may hold values from 0 to 95, as said below
- valid_counts: int32 [8], P(('groups', 'rep', 'section')), parts along dimension 0, may hold values from 128 to 512, as said below
Outputs:
- fresh_embed: bfloat16 [8, 12, 1536], P(('groups', 'rep', 'section'), 'slide'), parts along dimension 0
- context: bfloat16 [8, 512, 1024], P(('groups', 'rep', 'section'), 'slide'), parts along dimension 0
There are 2 independent parts, one for each index of `groups`. A program takes and returns all parts, laid end to end along the dimension named above; an argument that names none is the same for every part. Nothing has to cross between parts.
Inputs may be any that keep to these rules, and one draw needn't show every extreme that they name: `tile_coords`: each slide's 512 positions sit on distinct cells of a 96 by 96 grid, in raster order (by y, then x); the cells (0, 0) and (95, 95) are always among them. `valid_counts`: positions at or beyond a slide's count are padding.
All inputs are finite; a program needn't handle non-finite values.
Results may differ from a plain program's by a relative error of at most 0.0078.
Values may be sent and summed in bfloat16 or wider, within the bound.
No kernel may reach another device: no remote copies, remote signals or barrier semaphores. Data moves between devices by JAX's collectives and lax.ppermute only.
A program may use at most 64 MiB of HBM per device.

v0:
```python
import math
import jax
import jax.numpy as jnp
from jax import lax
from jax.sharding import PartitionSpec as P

SIDE = 7
KER = 7
HDIM = 64


def layer_norm(inputs, gain, shift, epsilon):
    center = jnp.mean(inputs, axis=-1, keepdims=True)
    centered = inputs - center
    spread = jnp.mean(centered * centered, axis=-1, keepdims=True)
    return centered * lax.rsqrt(spread + epsilon) * gain + shift


def depthwise(tile_data, depth_weight, depth_bias):
    tile_count = tile_data.shape[0]
    channels = tile_data.shape[-1]
    spatial = tile_data.reshape(tile_count, SIDE, SIDE, channels)
    margin = KER // 2
    padded = jnp.pad(spatial, ((0, 0), (margin, margin), (margin, margin), (0, 0)))
    running = jnp.zeros_like(spatial) + depth_bias
    for tap_row in range(KER):
        for tap_col in range(KER):
            running = (
                running
                + padded[:, tap_row : tap_row + SIDE, tap_col : tap_col + SIDE, :]
                * depth_weight[tap_row * KER + tap_col]
            )
    return running.reshape(tile_count, SIDE * SIDE, channels)


def normalize_heads(values):
    row_total = values.shape[0]
    grouped = values.reshape(row_total, -1, 3, HDIM)
    paired = grouped[:, :, :2]
    scaled = paired * lax.rsqrt(jnp.mean(paired * paired, axis=-1, keepdims=True) + 1e-06)
    joined = jnp.concatenate([scaled, grouped[:, :, 2:]], axis=2)
    return joined.astype(jnp.bfloat16).reshape(row_total, -1)


def on_device(
    tile_features,
    depth_weight,
    depth_bias,
    norm_gain,
    norm_bias,
    up_weight,
    up_bias,
    down_weight,
    down_bias,
    layer_scale,
    head_gain,
    head_bias,
    embed_store,
    in_weight,
    slide_gain,
    qkv_weight,
    head_slopes,
    tile_coords,
    valid_counts,
):
    tile_data = tile_features[0].astype(jnp.float32)
    fresh_count = tile_data.shape[0]
    channels = tile_data.shape[-1]
    convolved = depthwise(tile_data, depth_weight, depth_bias)
    normed = (
        layer_norm(convolved, norm_gain, norm_bias, 1e-06)
        .astype(jnp.bfloat16)
        .reshape(-1, channels)
    )
    hidden = jax.nn.gelu(
        jnp.dot(
            lax.all_gather(normed, "rep", axis=0, tiled=True),
            up_weight,
            preferred_element_type=jnp.float32,
        )
        + up_bias,
        approximate=False,
    ).astype(jnp.bfloat16)
    summed = lax.psum_scatter(
        jnp.dot(hidden, down_weight, preferred_element_type=jnp.float32).astype(jnp.bfloat16),
        "rep",
        scatter_dimension=0,
        tiled=True,
    ).astype(jnp.float32)
    updated = tile_data + layer_scale * (summed.reshape(tile_data.shape) + down_bias)
    pooled = jnp.mean(updated, axis=1)
    embedded = layer_norm(pooled, head_gain, head_bias, 1e-06).astype(jnp.bfloat16)
    seq_rows = jnp.concatenate([embedded, embed_store[0, fresh_count:]], axis=0)
    projected = jnp.dot(
        seq_rows,
        lax.all_gather(in_weight, "slide", axis=0, tiled=True),
        preferred_element_type=jnp.float32,
    )
    normed_seq = layer_norm(projected, slide_gain, 0.0, 1e-05).astype(jnp.bfloat16)
    full_weight = lax.all_gather(qkv_weight, "slide", axis=1, tiled=True)
    packed = normalize_heads(jnp.dot(normed_seq, full_weight, preferred_element_type=jnp.float32))
    local_heads = lax.all_to_all(packed, "slide", split_axis=1, concat_axis=0, tiled=True)
    seq_len = local_heads.shape[0]
    heads_here = local_heads.shape[1] // (3 * HDIM)
    arranged = local_heads.reshape(seq_len, heads_here, 3, HDIM)
    queries = arranged[:, :, 0]
    key_rows = arranged[:, :, 1]
    value_rows = arranged[:, :, 2]
    my_slopes = lax.dynamic_slice_in_dim(
        head_slopes, lax.axis_index("slide") * heads_here, heads_here, 0
    )
    coord_x = tile_coords[0, 0].astype(jnp.float32)
    coord_y = tile_coords[0, 1].astype(jnp.float32)
    valid = valid_counts[0]
    key_ok = jnp.arange(seq_len, dtype=jnp.int32) < valid
    inv_root = 1.0 / math.sqrt(HDIM)
    block_len = min(512, seq_len)
    block_count = seq_len // block_len

    def one_block(block_index):
        first_row = block_index * block_len
        query_block = lax.dynamic_slice_in_dim(queries, first_row, block_len, 0)
        query_x = lax.dynamic_slice_in_dim(coord_x, first_row, block_len, 0)
        query_y = lax.dynamic_slice_in_dim(coord_y, first_row, block_len, 0)
        distance = jnp.abs(query_x[:, None] - coord_x[None, :]) + jnp.abs(
            query_y[:, None] - coord_y[None, :]
        )
        scores = (
            jnp.einsum("qhd,khd->hqk", query_block, key_rows, preferred_element_type=jnp.float32)
            * inv_root
            - my_slopes[:, None, None] * distance[None]
        )
        weights = jnp.where(key_ok[None, None, :], jnp.exp(scores), 0.0).astype(jnp.bfloat16)
        totals = jnp.sum(weights, axis=-1, dtype=jnp.float32)
        weighted = jnp.einsum(
            "hqk,khd->qhd", weights, value_rows, preferred_element_type=jnp.float32
        )
        query_ok = first_row + jnp.arange(block_len, dtype=jnp.int32) < valid
        safe = jnp.where(query_ok[None, :], totals, 1.0)
        result = jnp.where(query_ok[:, None, None], weighted / safe.T[:, :, None], 0.0)
        return result.astype(jnp.bfloat16).reshape(block_len, heads_here * HDIM)

    attended = lax.map(one_block, jnp.arange(block_count, dtype=jnp.int32)).reshape(
        seq_len, heads_here * HDIM
    )
    context = lax.all_to_all(attended, "slide", split_axis=0, concat_axis=1, tiled=True)
    return (embedded[None], context[None])


def solution(mesh):
    in_specs = (
        P(("groups", "rep", "section"), "slide", None, None),
        P(),
        P(),
        P(),
        P(),
        P(None, "rep"),
        P("rep"),
        P("rep", None),
        P(),
        P(),
        P(),
        P(),
        P(("groups", "rep", "section"), "slide", None),
        P("slide", None),
        P(),
        P(None, "slide"),
        P(),
        P(("groups", "rep", "section"), None, None),
        P(("groups", "rep", "section")),
    )
    out_specs = (
        P(("groups", "rep", "section"), "slide", None),
        P(("groups", "rep", "section"), "slide", None),
    )
    return jax.shard_map(
        on_device, mesh=mesh, in_specs=in_specs, out_specs=out_specs, check_vma=False
    )
```

profile of v0, /device:TPU:0, one launch (start us, length us, event | category | flops | bytes accessed | tf_op | source)
XLA Modules:
  0.0 245.6 jit_solution(2592706791371269726)
XLA Ops:
  7.2 0.0 all-gather.4.cloned.1.call-start
  7.2 0.7 all-gather.4.cloned.1.call-update
  7.9 0.0 all-gather.6.cloned.1.call-start
  8.0 0.7 all-gather.6.cloned.1.call-update
  8.7 0.1 reshape.371
  8.8 0.2 slice_reduce_fusion.46
  9.0 0.3 slice_reduce_fusion.47
  9.3 0.3 slice_reduce_fusion.48
  9.7 7.9 %fusion.187 = (f32[3,7,7]{2,1,0:T(8,128)S(1)}, f32[3,7,7,1536]{3,2,1,0:T(8,128)S(1)}) fusion(f32[1536]{0:T(1024)S(1)} %get-tuple-element.81, f32[1536]{0:T(1024)S(1)} %get-tuple-element.82, f32[1536]{0:T(1024)S(1)} %get-tuple-element.25, f32[1536]{0:T(1024)S(1)} %get-tuple-element.26, f32[1536]{0:T(1024)S(1)} %get-tuple-element.27, ...), kind=kLoop, calls=%fused_computation.327 | loop fusion | flops 22353260 | bytes 2114124 | tf_op jit(solution)/shard_map/reduce_sum | solution.py:13
  17.6 0.1 reshape.365
  17.7 0.1 div.47
  17.8 0.3 multiply_reduce_fusion.1
  18.1 0.1 rsqrt.36
  18.2 0.1 copy-done.6
  18.3 0.0 copy-done.7
  18.3 0.2 fusion.143
  18.5 0.0 copy-start.13
  18.5 14.3 %all-gather = bf16[2,147,1536]{2,1,0:T(8,128)(2,1)S(1)} all-gather(bf16[1,147,1536]{2,1,0:T(8,128)(2,1)S(1)} %fusion.143), channel_id=1, replica_groups=mesh['groups'=2,'slide'=4,'rep'=2,'section'=2] {'rep'}, dimensions={0}, use_global_device_ids=true | all-gather | bytes 1354752 | tf_op jit(solution)/shard_map/all_gather | solution.py:77
  32.8 0.2 reshape.375
  33.0 0.0 copy-start.1
  33.0 10.5 %convolution_convert_fusion = bf16[294,1536]{1,0:T(8,128)(2,1)S(1)} fusion(bf16[1536,1536]{1,0:T(8,128)(2,1)} %param.26, bf16[294,1536]{1,0:T(8,128)(2,1)S(1)} %reshape.375, bf16[1536,1536]{1,0:T(8,128)(2,1)} %param.24, f32[1536]{0:T(1024)S(1)} %copy-done.13), kind=kOutput, calls=%fused_computation.52 | convolution fusion | flops 2804788224 | bytes 11249664 | tf_op jit(solution)/shard_map/dot_general | solution.py:85
  43.6 0.0 copy-start.12
  43.6 14.9 %fusion = bf16[152,1536]{1,0:T(8,128)(2,1)S(1)} fusion(bf16[294,1536]{1,0:T(8,128)(2,1)S(1)} %convolution_convert_fusion), kind=kCustom, calls=%all-reduce-scatter | all-reduce-scatter fusion | flops 466945 | bytes 1370624
  58.6 2.7 %collective-permute-start = (bf16[5,1536]{1,0:T(8,128)(2,1)S(1)}, bf16[5,1536]{1,0:T(8,128)(2,1)S(1)}, u32[]{:S(2)}, u32[]{:S(2)}) collective-permute-start(bf16[5,1536]{1,0:T(8,128)(2,1)S(1)} %slice.427), channel_id=1, source_target_pairs={{0,2},{1,3},{4,6},{5,7},{8,10},{9,11},{12,14},{13,15},{16,18},{17,... | collective-permute-start | bytes 46088
  61.3 0.1 slice_bitcast_fusion
  61.4 0.6 dynamic-slice.4
  62.6 0.6 concatenate.9
  63.2 0.0 copy-start.8
  63.2 0.0 copy-start.9
  63.2 0.1 dynamic-slice_convert_fusion
  63.4 0.0 copy-start.3
  63.4 0.0 copy-start.4
  63.4 0.1 reshape.373
  63.5 0.4 copy-done.8
  63.9 0.0 copy-done.9
  63.9 0.2 fusion.111
  64.1 0.1 multiply_reduce_fusion.4
  64.3 0.2 multiply_reduce_fusion.3
  64.5 0.1 add_convert_fusion.1
  64.6 0.0 copy-start.10
  64.6 11.2 %all-gather.4.cloned.1.call-done = bf16[1536,1024]{1,0:T(8,128)(2,1)} async-done(((bf16[384,1024]{1,0:T(8,128)(2,1)}), bf16[1536,1024]{1,0:T(8,128)(2,1)}) %all-gather.4.cloned.1.call-update) | async-done | bytes 3145744 | tf_op jit(solution)/shard_map/all_gather | solution.py:96
  75.8 2.6 %fusion.189 = (f32[128]{0:T(128)S(1)}, f32[128,1024]{1,0:T(8,128)S(1)}) fusion(bf16[1536,1024]{1,0:T(8,128)(2,1)} %all-gather.4.cloned.1.call-done, bf16[125,1536]{1,0:T(8,128)(2,1)S(1)} %slice_bitcast_fusion, bf16[3,1536]{1,0:T(4,128)(2,1)S(1)} %add_convert_fusion.1), kind=kOutput, calls=%fused_computation.328 | convolution fusion | flops 403570560 | bytes 4063744 | tf_op jit(solution)/shard_map/dot_general | solution.py:94
  78.4 0.2 multiply_reduce_fusion.2
  78.6 112.8 %all-gather.6.cloned.1.call-done = bf16[1024,3072]{1,0:T(8,128)(2,1)} async-done(((bf16[1024,768]{1,0:T(8,128)(2,1)}), bf16[1024,3072]{1,0:T(8,128)(2,1)}) %all-gather.6.cloned.1.call-update) | async-done | bytes 6291472 | tf_op jit(solution)/shard_map/all_gather | solution.py:100
  191.4 5.4 %fusion.148 = f32[128,3072]{0,1:T(8,128)S(1)} fusion(bf16[1024,3072]{1,0:T(8,128)(2,1)} %all-gather.6.cloned.1.call-done, f32[128,1024]{1,0:T(8,128)S(1)} %get-tuple-element.88, f32[1024]{0:T(1024)S(1)} %copy-done.10, f32[128]{0:T(128)S(1)} %add_rsqrt_fusion.2, f32[128]{0:T(128)S(1)} %broadcast_multiply_fusion.1), kind=kOutput, calls=%fused_computation.221 | convolution fusion | flops 805830656 | bytes 8393728 | tf_op jit(solution)/shard_map/dot_general | solution.py:101
  196.9 0.1 multiply_reduce_fusion
  197.1 0.1 multiply_convert_fusion
  197.2 0.0 copy-start.14
  197.2 0.0 copy-start.11
  197.2 1.0 pad_maximum_fusion
  198.2 3.5 %all-to-all-start = ((bf16[128,4,768]{0,2,1:T(8,128)(2,1)}), bf16[128,4,768]{0,2,1:T(8,128)(2,1)S(1)}, u32[]{:S(2)}, u32[]{:S(2)}) async-start(bf16[128,4,768]{0,2,1:T(8,128)(2,1)} %bitcast.6), calls=%async_computation | async-start | bytes 1572864 | tf_op jit(solution)/shard_map/all_to_all | solution.py:102
  202.3 0.1 dynamic_slice.12
  202.4 0.2 abs_add_fusion
  202.7 19.6 %all-to-all-done = bf16[128,4,768]{0,2,1:T(8,128)(2,1)S(1)} async-done(((bf16[128,4,768]{0,2,1:T(8,128)(2,1)}), bf16[128,4,768]{0,2,1:T(8,128)(2,1)S(1)}, u32[]{:S(2)}, u32[]{:S(2)}) %all-to-all-start) | async-done | bytes 786464 | tf_op jit(solution)/shard_map/all_to_all | solution.py:102
  222.2 0.6 copy.31
  222.9 0.3 reshape.369
  223.2 1.5 convert_reduce_fusion
  224.7 0.5 fusion.13
  225.1 0.1 all_to_all.24
  225.2 0.7 copy.36
  225.9 3.4 %all-to-all-start.1 = ((bf16[4,128,256]{1,2,0:T(8,128)(2,1)}), bf16[4,128,256]{1,2,0:T(8,128)(2,1)S(1)}, u32[]{:S(2)}, u32[]{:S(2)}) async-start(bf16[4,128,256]{1,2,0:T(8,128)(2,1)} %copy.36), calls=%async_computation.1 | async-start | bytes 524288 | tf_op jit(solution)/shard_map/all_to_all | solution.py:146
  229.4 0.7 fusion.155
  230.0 7.8 %all-to-all-done.1 = bf16[4,128,256]{1,2,0:T(8,128)(2,1)S(1)} async-done(((bf16[4,128,256]{1,2,0:T(8,128)(2,1)}), bf16[4,128,256]{1,2,0:T(8,128)(2,1)S(1)}, u32[]{:S(2)}, u32[]{:S(2)}) %all-to-all-start.1) | async-done | bytes 262176 | tf_op jit(solution)/shard_map/all_to_all | solution.py:146
  237.9 0.8 copy.37
  (29 shorter events, 0.2 us)
Async XLA Ops:
  7.2 1.5 copy-start
  7.2 1.7 copy-start.2
  7.2 68.7 %all-gather.4.cloned.1.call-start = ((), (), s32[]{:S(2)}) async-start(), calls=%async_computation.2 | async-start | bytes 3932160 | tf_op jit(solution)/shard_map/all_gather | solution.py:96
  7.9 1.8 copy-start.5
  7.9 183.5 %all-gather.6.cloned.1.call-start = ((), (), s32[]{:S(2)}) async-start(), calls=%async_computation.3 | async-start | bytes 7864320 | tf_op jit(solution)/shard_map/all_gather | solution.py:100
  17.5 0.7 copy-start.6
  17.5 0.7 copy-start.7
  18.5 14.5 %copy-start.13 = (f32[1536]{0:T(1024)S(1)}, f32[1536]{0:T(1024)}, u32[]{:S(2)}) copy-start(f32[1536]{0:T(1024)} %param.25) | copy-start | bytes 18436
  33.0 28.2 %copy-start.1 = (bf16[1,128,1536]{2,1,0:T(8,128)(2,1)S(1)}, bf16[1,128,1536]{2,1,0:T(8,128)(2,1)}, u32[]{:S(2)}) copy-start(bf16[1,128,1536]{2,1,0:T(8,128)(2,1)} %param.31) | copy-start | bytes 1179652
  43.6 17.8 %copy-start.12 = (u32[32]{0:T(128)S(1)}, u32[32]{0:T(128)}, u32[]{:S(2)}) copy-start(u32[32]{0:T(128)} %constant.125) | copy-start | bytes 388
  58.6 4.1 %collective-permute-start = (bf16[5,1536]{1,0:T(8,128)(2,1)S(1)}, bf16[5,1536]{1,0:T(8,128)(2,1)S(1)}, u32[]{:S(2)}, u32[]{:S(2)}) collective-permute-start(bf16[5,1536]{1,0:T(8,128)(2,1)S(1)} %slice.427), channel_id=1, source_target_pairs={{0,2},{1,3},{4,6},{5,7},{8,10},{9,11},{12,14},{13,15},{16,18},{17,... | collective-permute-start | bytes 46088
  63.2 0.7 copy-start.8
  63.2 0.7 copy-start.9
  63.4 1.1 copy-start.3
  63.4 1.1 copy-start.4
  64.6 126.9 %copy-start.10 = (f32[1024]{0:T(1024)S(1)}, f32[1024]{0:T(1024)}, u32[]{:S(2)}) copy-start(f32[1024]{0:T(1024)} %param.33) | copy-start | bytes 12292
  197.2 5.1 %copy-start.14 = (f32[16]{0:T(128)S(1)}, f32[16]{0:T(128)}, u32[]{:S(2)}) copy-start(f32[16]{0:T(128)} %param.35) | copy-start | bytes 196
  197.2 5.2 %copy-start.11 = (s32[1,2,512]{2,1,0:T(2,128)S(1)}, s32[1,2,512]{2,1,0:T(2,128)}, u32[]{:S(2)}) copy-start(s32[1,2,512]{2,1,0:T(2,128)} %param.36) | copy-start | bytes 12292
  198.2 24.1 %all-to-all-start = ((bf16[128,4,768]{0,2,1:T(8,128)(2,1)}), bf16[128,4,768]{0,2,1:T(8,128)(2,1)S(1)}, u32[]{:S(2)}, u32[]{:S(2)}) async-start(bf16[128,4,768]{0,2,1:T(8,128)(2,1)} %bitcast.6), calls=%async_computation | async-start | bytes 1572864 | tf_op jit(solution)/shard_map/all_to_all | solution.py:102
  225.9 11.9 %all-to-all-start.1 = ((bf16[4,128,256]{1,2,0:T(8,128)(2,1)}), bf16[4,128,256]{1,2,0:T(8,128)(2,1)S(1)}, u32[]{:S(2)}, u32[]{:S(2)}) async-start(bf16[4,128,256]{1,2,0:T(8,128)(2,1)} %copy.36), calls=%async_computation.1 | async-start | bytes 524288 | tf_op jit(solution)/shard_map/all_to_all | solution.py:146
Sparse Core Ops, SparseCore 0:
  9.6 66.2 all-gather.3
  77.4 113.9 all-gather.5
where the time goes:
time: 246 us
  waiting for transfers between devices  153 us (62%)
  blocking collectives  29.3 us (12%)
  matrix products  20.5 us (8%)
  between operations  15.7 us (6%)
  other arithmetic  11.5 us (5%)
  starting transfers between devices  9.67 us (4%)
  local copies, waits for them, and re-layouts  6.05 us (2%)
    all_gather x1, waiting for transfers between devices, on_device(): full_weight = lax.all_gather(qkv_weight, 'slide', axis=1, tiled=True)  113 us
    all_to_all x1, waiting for transfers between devices, on_device(): lax.all_to_all(packed, 'slide', split_axis=1, concat_axis=0, tiled=True)  19.6 us
    unnamed x1, blocking collectives  14.9 us
    all_gather x1, blocking collectives, on_device(): lax.all_gather(normed, 'rep', axis=0, tiled=True)  14.3 us
    all_gather x1, waiting for transfers between devices, on_device(): lax.all_gather(in_weight, 'slide', axis=0, tiled=True)  11.2 us
    dot_general x1, matrix products, on_device(): jnp.dot(hidden, down_weight, preferred_element_type=jnp.float32)  10.5 us
    reduce_sum x2, other arithmetic, layer_norm(): center = jnp.mean(inputs, axis=-1, keepdims=True)  8 us
    all_to_all x1, waiting for transfers between devices, on_device(): lax.all_to_all(attended, 'slide', split_axis=0, concat_axis=1, tiled=True)  7.82 us
  transfers between devices with their start and end apart: 5, of which 4 were waited for; matrix products, arithmetic and copies ran while one was open for 17% of the time, Pallas kernels for 0%

commit v1 on v0

--- a/solution.py
+++ b/solution.py
@@ -97,7 +97,14 @@
         preferred_element_type=jnp.float32,
     )
     normed_seq = layer_norm(projected, slide_gain, 0.0, 1e-05).astype(jnp.bfloat16)
-    full_weight = lax.all_gather(qkv_weight, "slide", axis=1, tiled=True)
+    ring = [qkv_weight]
+    for hop in range(3):
+        ring.append(lax.ppermute(ring[-1], "slide", [(dev, (dev + 1) % 4) for dev in range(4)]))
+    full_weight = jnp.roll(
+        jnp.concatenate(ring[::-1], axis=1),
+        (lax.axis_index("slide") + 1) * ring[0].shape[1],
+        axis=1,
+    )
     packed = normalize_heads(jnp.dot(normed_seq, full_weight, preferred_element_type=jnp.float32))
     local_heads = lax.all_to_all(packed, "slide", split_axis=1, concat_axis=0, tiled=True)
     seq_len = local_heads.shape[0]

time: 246 us -> 226 us (0.919)
  waiting for transfers between devices: 153 us -> 74.1 us
  starting transfers between devices: 9.67 us -> 35.7 us
  other arithmetic: 11.5 us -> 31.5 us
  local copies, waits for them, and re-layouts: 6.05 us -> 20.2 us
  blocking collectives: 29.3 us -> 25.8 us
    all_gather x1 -> x0, waiting for transfers between devices: 113 us -> none  [on_device(): full_weight = lax.all_gather(qkv_weight, 'slide', axis=1, tiled=True)]
    ppermute x0 -> x3, waiting for transfers between devices: none -> 52.1 us  [on_device(): lax.ppermute(ring[-1], 'slide', [(dev, (dev + 1) % 4) for dev in range(4)])]
    ppermute x0 -> x3, starting transfers between devices: none -> 26.2 us  [on_device(): lax.ppermute(ring[-1], 'slide', [(dev, (dev + 1) % 4) for dev in range(4)])]
    reduce_sum x2, other arithmetic: 8 us -> 24.9 us  [layer_norm(): center = jnp.mean(inputs, axis=-1, keepdims=True)]
    all_gather x1, waiting for transfers between devices: 11.2 us -> 0.02 us  [on_device(): lax.all_gather(in_weight, 'slide', axis=0, tiled=True)]
    unnamed x35 -> x36, local copies, waits for them, and re-layouts: 2.75 us -> 11 us
    all_to_all x1, waiting for transfers between devices: 19.6 us -> 15.2 us  [on_device(): lax.all_to_all(packed, 'slide', split_axis=1, concat_axis=0, tiled=True)]
    slice x3, local copies, waits for them, and re-layouts: 0.82 us -> 4.82 us  [depthwise(): depth_weight[tap_row * KER + tap_col]]
  transfers between devices with their start and end apart: 5 -> 7, of which waited for: 4 -> 5; matrix products, arithmetic and copies ran while one was open for 17% -> 29% of each run, Pallas kernels for 0% -> 0%
where the time goes in v1:
time: 226 us; the launch traced here: 225 us
  waiting for transfers between devices  74.1 us (33%)
  starting transfers between devices  35.7 us (16%)
  other arithmetic  31.5 us (14%)
  blocking collectives  25.8 us (11%)
  matrix products  21.5 us (10%)
  local copies, waits for them, and re-layouts  20.2 us (9%)
  between operations  15.8 us (7%)
    ppermute x3, waiting for transfers between devices, on_device(): lax.ppermute(ring[-1], 'slide', [(dev, (dev + 1) % 4) for dev in range(4)])  52.1 us
    ppermute x3, starting transfers between devices, on_device(): lax.ppermute(ring[-1], 'slide', [(dev, (dev + 1) % 4) for dev in range(4)])  26.2 us
    reduce_sum x2, other arithmetic, layer_norm(): center = jnp.mean(inputs, axis=-1, keepdims=True)  24.9 us
    all_to_all x1, waiting for transfers between devices, on_device(): lax.all_to_all(packed, 'slide', split_axis=1, concat_axis=0, tiled=True)  15.2 us
    all_gather x1, blocking collectives, on_device(): lax.all_gather(normed, 'rep', axis=0, tiled=True)  13 us
    unnamed x1, blocking collectives  12.8 us
    dot_general x1, matrix products, on_device(): jnp.dot(hidden, down_weight, preferred_element_type=jnp.float32)  11.4 us
    unnamed x36, local copies, waits for them, and re-layouts  11 us
  transfers between devices with their start and end apart: 7, of which 5 were waited for; matrix products, arithmetic and copies ran while one was open for 29% of the time, Pallas kernels for 0%

profile of v1, /device:TPU:0, one launch (start us, length us, event | category | flops | bytes accessed | tf_op | source)
XLA Modules:
  0.0 224.6 jit_solution(17833632522492874080)
XLA Ops:
  7.2 0.0 all-gather.3.cloned.1.call-start
  7.2 0.7 all-gather.3.cloned.1.call-update
  7.9 3.1 %collective-permute-start = (bf16[1024,768]{1,0:T(8,128)(2,1)}, bf16[1024,768]{1,0:T(8,128)(2,1)S(1)}, u32[]{:S(2)}, u32[]{:S(2)}) collective-permute-start(bf16[1024,768]{1,0:T(8,128)(2,1)} %param.34), channel_id=1, source_target_pairs={{0,4},{4,8},{8,12},{12,0},{1,5},{5,9},{9,13},{13,1},{2,6},{6,10},{... | collective-permute-start | bytes 4718600 | tf_op jit(solution)/shard_map/ppermute | solution.py:102
  11.0 1.8 slice_reduce_fusion.48
  12.8 1.7 slice_reduce_fusion.47
  14.6 1.3 slice_reduce_fusion.46
  15.8 1.1 reshape.371
  16.9 24.7 %fusion.189 = (f32[3,7,7]{2,1,0:T(8,128)S(1)}, f32[3,7,7,1536]{3,2,1,0:T(8,128)S(1)}) fusion(f32[1536]{0:T(1024)S(1)} %get-tuple-element.81, f32[1536]{0:T(1024)S(1)} %get-tuple-element.82, f32[1536]{0:T(1024)S(1)} %get-tuple-element.25, f32[1536]{0:T(1024)S(1)} %get-tuple-element.26, f32[1536]{0:T(1024)S(1)} %get-tuple-element.27, ...), kind=kLoop, calls=%fused_computation.337 | loop fusion | flops 22353260 | bytes 2114124 | tf_op jit(solution)/shard_map/reduce_sum | solution.py:13
  41.7 0.1 reshape.365
  41.8 0.9 multiply_reduce_fusion.1
  42.7 0.1 div.47
  42.8 0.7 add_rsqrt_fusion.1
  43.5 0.1 rsqrt.36
  43.6 0.9 fusion.145
  44.6 13.0 %all-gather = bf16[2,147,1536]{2,1,0:T(8,128)(2,1)S(1)} all-gather(bf16[1,147,1536]{2,1,0:T(8,128)(2,1)S(1)} %fusion.145), channel_id=1, replica_groups=mesh['groups'=2,'slide'=4,'rep'=2,'section'=2] {'rep'}, dimensions={0}, use_global_device_ids=true | all-gather | bytes 1354752 | tf_op jit(solution)/shard_map/all_gather | solution.py:77
  57.6 0.2 reshape.375
  57.8 0.0 copy-start.3
  57.8 11.4 %convolution_convert_fusion = bf16[294,1536]{1,0:T(8,128)(2,1)} fusion(bf16[1536,1536]{1,0:T(8,128)(2,1)} %param.26, bf16[294,1536]{1,0:T(8,128)(2,1)S(1)} %reshape.375, bf16[1536,1536]{1,0:T(8,128)(2,1)} %param.24, f32[1536]{0:T(1024)S(1)} %copy-done.10), kind=kOutput, calls=%fused_computation.54 | convolution fusion | flops 2804788224 | bytes 11249664 | tf_op jit(solution)/shard_map/dot_general | solution.py:85
  69.3 2.0 collective-permute-done
  71.2 23.1 %collective-permute-start.1 = (bf16[1024,768]{1,0:T(8,128)(2,1)S(1)}, bf16[1024,768]{1,0:T(8,128)(2,1)}, u32[]{:S(2)}, u32[]{:S(2)}) collective-permute-start(bf16[1024,768]{1,0:T(8,128)(2,1)S(1)} %collective-permute-done), channel_id=1, source_target_pairs={{0,4},{4,8},{8,12},{12,0},{1,5},{5,9},{9,13},{13,1},{2,6},{6,10},{... | collective-permute-start | bytes 4718600 | tf_op jit(solution)/shard_map/ppermute | solution.py:102
  94.3 12.8 %fusion = bf16[152,1536]{1,0:T(8,128)(2,1)S(1)} fusion(bf16[294,1536]{1,0:T(8,128)(2,1)} %convolution_convert_fusion), kind=kCustom, calls=%all-reduce-scatter | all-reduce-scatter fusion | flops 466945 | bytes 1370624
  107.1 2.6 %collective-permute-start.3 = (bf16[5,1536]{1,0:T(8,128)(2,1)S(1)}, bf16[5,1536]{1,0:T(8,128)(2,1)S(1)}, u32[]{:S(2)}, u32[]{:S(2)}) collective-permute-start(bf16[5,1536]{1,0:T(8,128)(2,1)S(1)} %slice.427), channel_id=1, source_target_pairs={{0,2},{1,3},{4,6},{5,7},{8,10},{9,11},{12,14},{13,15},{16,18},{17,... | collective-permute-start | bytes 46088
  109.7 0.9 slice_bitcast_fusion
  110.6 0.6 dynamic-slice.4
  111.9 0.6 concatenate.16
  112.4 0.1 dynamic-slice_convert_fusion
  112.6 0.1 reshape.373
  112.7 1.3 fusion.113
  114.0 0.1 multiply_reduce_fusion.4
  114.2 0.2 multiply_reduce_fusion.3
  114.4 18.0 %collective-permute-done.1 = bf16[1024,768]{1,0:T(8,128)(2,1)} collective-permute-done((bf16[1024,768]{1,0:T(8,128)(2,1)S(1)}, bf16[1024,768]{1,0:T(8,128)(2,1)}, u32[]{:S(2)}, u32[]{:S(2)}) %collective-permute-start.1) | collective-permute-done | bytes 1572896 | tf_op jit(solution)/shard_map/ppermute | solution.py:102
  132.4 0.1 add_convert_fusion.1
  132.5 0.0 all-gather.3.cloned.1.call-done
  132.5 2.5 %fusion.191 = (f32[128]{0:T(128)S(1)}, f32[128,1024]{1,0:T(8,128)S(1)}) fusion(bf16[1536,1024]{1,0:T(8,128)(2,1)} %all-gather.3.cloned.1.call-done, bf16[125,1536]{1,0:T(8,128)(2,1)S(1)} %copy-done.2, bf16[3,1536]{1,0:T(4,128)(2,1)S(1)} %add_convert_fusion.1), kind=kOutput, calls=%fused_computation.338 | convolution fusion | flops 403570560 | bytes 4063744 | tf_op jit(solution)/shard_map/dot_general | solution.py:94
  135.1 0.2 multiply_reduce_fusion.2
  135.3 32.1 %collective-permute-done.2 = bf16[1024,768]{1,0:T(8,128)(2,1)} collective-permute-done((bf16[1024,768]{1,0:T(8,128)(2,1)}, bf16[1024,768]{1,0:T(8,128)(2,1)}, u32[]{:S(2)}, u32[]{:S(2)}) %collective-permute-start.2) | collective-permute-done | bytes 1572896 | tf_op jit(solution)/shard_map/ppermute | solution.py:102
  167.4 1.6 constant_dynamic-update-slice_fusion.7
  169.0 1.6 constant_dynamic-update-slice_fusion.6
  170.7 0.2 constant_dynamic-update-slice_fusion.5
  170.9 1.2 copy-done
  172.1 0.2 constant_dynamic-update-slice_fusion.4
  172.3 1.6 constant_dynamic-update-slice_fusion.3
  173.9 1.6 constant_dynamic-update-slice_fusion.2
  175.5 0.2 constant_dynamic-update-slice_fusion.1
  175.8 0.2 constant_dynamic-update-slice_fusion
  176.0 0.5 copy-done.7
  176.5 5.6 %fusion.1 = f32[128,3072]{0,1:T(8,128)S(1)} fusion(bf16[1024,6144]{1,0:T(8,128)(2,1)S(1)} %constant_dynamic-update-slice_fusion, s32[]{:T(128)S(6)} %select_n.40, f32[128,1024]{1,0:T(8,128)S(1)} %get-tuple-element.88, f32[1024]{0:T(1024)S(1)} %copy-done.7, f32[128]{0:T(128)S(1)} %add_rsqrt_fusion.2, f32[128]{0:T(128)S(1)} %broadcast_multiply_fusion.1), kind=kOutput, calls=%fused_computation.48 | convolution fusion | flops 805830656 | bytes 8393732 | tf_op jit(solution)/shard_map/dot_general | solution.py:108
  182.0 0.1 multiply_reduce_fusion
  182.2 0.1 multiply_convert_fusion
  182.4 1.0 pad_maximum_fusion
  183.3 3.5 %all-to-all-start = ((bf16[128,4,768]{0,2,1:T(8,128)(2,1)}), bf16[128,4,768]{0,2,1:T(8,128)(2,1)S(1)}, u32[]{:S(2)}, u32[]{:S(2)}) async-start(bf16[128,4,768]{0,2,1:T(8,128)(2,1)} %bitcast.6), calls=%async_computation | async-start | bytes 1572864 | tf_op jit(solution)/shard_map/all_to_all | solution.py:109
  187.5 0.1 dynamic_slice.17
  187.6 0.2 abs_add_fusion
  187.8 15.2 %all-to-all-done = bf16[128,4,768]{0,2,1:T(8,128)(2,1)S(1)} async-done(((bf16[128,4,768]{0,2,1:T(8,128)(2,1)}), bf16[128,4,768]{0,2,1:T(8,128)(2,1)S(1)}, u32[]{:S(2)}, u32[]{:S(2)}) %all-to-all-start) | async-done | bytes 786464 | tf_op jit(solution)/shard_map/all_to_all | solution.py:109
  203.1 0.6 copy.31
  203.7 0.3 reshape.369
  204.0 1.5 convert_reduce_fusion
  205.5 0.5 fusion.15
  205.9 0.1 all_to_all.24
  206.0 0.7 copy.36
  206.8 3.4 %all-to-all-start.1 = ((bf16[4,128,256]{1,2,0:T(8,128)(2,1)}), bf16[4,128,256]{1,2,0:T(8,128)(2,1)S(1)}, u32[]{:S(2)}, u32[]{:S(2)}) async-start(bf16[4,128,256]{1,2,0:T(8,128)(2,1)} %copy.36), calls=%async_computation.1 | async-start | bytes 524288 | tf_op jit(solution)/shard_map/all_to_all | solution.py:153
  210.2 0.7 fusion.156
  210.8 6.1 %all-to-all-done.1 = bf16[4,128,256]{1,2,0:T(8,128)(2,1)S(1)} async-done(((bf16[4,128,256]{1,2,0:T(8,128)(2,1)}), bf16[4,128,256]{1,2,0:T(8,128)(2,1)S(1)}, u32[]{:S(2)}, u32[]{:S(2)}) %all-to-all-start.1) | async-done | bytes 262176 | tf_op jit(solution)/shard_map/all_to_all | solution.py:153
  216.9 0.8 copy.37
  (34 shorter events, 0.2 us)
Async XLA Ops:
  7.2 8.7 %copy-start.1 = (bf16[1,3,49,1536]{3,2,1,0:T(8,128)(2,1)S(1)}, bf16[1,3,49,1536]{3,2,1,0:T(8,128)(2,1)}, u32[]{:S(2)}) copy-start(bf16[1,3,49,1536]{3,2,1,0:T(8,128)(2,1)} %param.19) | copy-start | bytes 1354756
  7.2 9.8 %copy-start.6 = (f32[1536]{0:T(1024)S(1)}, f32[1536]{0:T(1024)}, u32[]{:S(2)}) copy-start(f32[1536]{0:T(1024)} %param.21) | copy-start | bytes 18436
  7.2 125.3 %all-gather.3.cloned.1.call-start = ((), (), s32[]{:S(2)}) async-start(), calls=%async_computation.2 | async-start | bytes 3932160 | tf_op jit(solution)/shard_map/all_gather | solution.py:96
  7.9 63.3 %collective-permute-start = (bf16[1024,768]{1,0:T(8,128)(2,1)}, bf16[1024,768]{1,0:T(8,128)(2,1)S(1)}, u32[]{:S(2)}, u32[]{:S(2)}) collective-permute-start(bf16[1024,768]{1,0:T(8,128)(2,1)} %param.34), channel_id=1, source_target_pairs={{0,4},{4,8},{8,12},{12,0},{1,5},{5,9},{9,13},{13,1},{2,6},{6,10},{... | collective-permute-start | bytes 4718600 | tf_op jit(solution)/shard_map/ppermute | solution.py:102
  44.6 13.2 %copy-start.10 = (f32[1536]{0:T(1024)S(1)}, f32[1536]{0:T(1024)}, u32[]{:S(2)}) copy-start(f32[1536]{0:T(1024)} %param.25) | copy-start | bytes 18436
  57.8 51.9 %copy-start.3 = (bf16[1,128,1536]{2,1,0:T(8,128)(2,1)S(1)}, bf16[1,128,1536]{2,1,0:T(8,128)(2,1)}, u32[]{:S(2)}) copy-start(bf16[1,128,1536]{2,1,0:T(8,128)(2,1)} %param.31) | copy-start | bytes 1179652
  69.3 41.4 %copy-start.9 = (u32[32]{0:T(128)S(1)}, u32[32]{0:T(128)}, u32[]{:S(2)}) copy-start(u32[32]{0:T(128)} %constant.147) | copy-start | bytes 388
  71.2 61.1 %collective-permute-start.1 = (bf16[1024,768]{1,0:T(8,128)(2,1)S(1)}, bf16[1024,768]{1,0:T(8,128)(2,1)}, u32[]{:S(2)}, u32[]{:S(2)}) collective-permute-start(bf16[1024,768]{1,0:T(8,128)(2,1)S(1)} %collective-permute-done), channel_id=1, source_target_pairs={{0,4},{4,8},{8,12},{12,0},{1,5},{5,9},{9,13},{13,1},{2,6},{6,10},{... | collective-permute-start | bytes 4718600 | tf_op jit(solution)/shard_map/ppermute | solution.py:102
  107.1 4.7 %collective-permute-start.3 = (bf16[5,1536]{1,0:T(8,128)(2,1)S(1)}, bf16[5,1536]{1,0:T(8,128)(2,1)S(1)}, u32[]{:S(2)}, u32[]{:S(2)}) collective-permute-start(bf16[5,1536]{1,0:T(8,128)(2,1)S(1)} %slice.427), channel_id=1, source_target_pairs={{0,2},{1,3},{4,6},{5,7},{8,10},{9,11},{12,14},{13,15},{16,18},{17,... | collective-permute-start | bytes 46088
  112.6 19.8 %copy-start.4 = (f32[1536]{0:T(1024)S(1)}, f32[1536]{0:T(1024)}, u32[]{:S(2)}) copy-start(f32[1536]{0:T(1024)} %param.30) | copy-start | bytes 18436
  112.6 19.8 %copy-start.5 = (f32[1536]{0:T(1024)S(1)}, f32[1536]{0:T(1024)}, u32[]{:S(2)}) copy-start(f32[1536]{0:T(1024)} %param.29) | copy-start | bytes 18436
  112.7 19.8 %copy-start.2 = (bf16[125,1536]{1,0:T(8,128)(2,1)S(1)}, bf16[125,1536]{1,0:T(8,128)(2,1)}, u32[]{:S(2)}) copy-start(bf16[125,1536]{1,0:T(8,128)(2,1)} %slice_bitcast_fusion) | copy-start | bytes 1152004
  132.3 35.1 %collective-permute-start.2 = (bf16[1024,768]{1,0:T(8,128)(2,1)}, bf16[1024,768]{1,0:T(8,128)(2,1)}, u32[]{:S(2)}, u32[]{:S(2)}) collective-permute-start(bf16[1024,768]{1,0:T(8,128)(2,1)} %collective-permute-done.1), channel_id=1, source_target_pairs={{0,4},{4,8},{8,12},{12,0},{1,5},{5,9},{9,13},{13,1},{2,6},{6,10},{... | collective-permute-start | bytes 4718600 | tf_op jit(solution)/shard_map/ppermute | solution.py:102
  170.7 1.4 copy-start
  175.8 0.7 copy-start.7
  182.3 5.1 %copy-start.11 = (f32[16]{0:T(128)S(1)}, f32[16]{0:T(128)}, u32[]{:S(2)}) copy-start(f32[16]{0:T(128)} %param.35) | copy-start | bytes 196
  182.4 5.2 %copy-start.8 = (s32[1,2,512]{2,1,0:T(2,128)S(1)}, s32[1,2,512]{2,1,0:T(2,128)}, u32[]{:S(2)}) copy-start(s32[1,2,512]{2,1,0:T(2,128)} %param.36) | copy-start | bytes 12292
  183.3 19.7 %all-to-all-start = ((bf16[128,4,768]{0,2,1:T(8,128)(2,1)}), bf16[128,4,768]{0,2,1:T(8,128)(2,1)S(1)}, u32[]{:S(2)}, u32[]{:S(2)}) async-start(bf16[128,4,768]{0,2,1:T(8,128)(2,1)} %bitcast.6), calls=%async_computation | async-start | bytes 1572864 | tf_op jit(solution)/shard_map/all_to_all | solution.py:109
  206.8 10.2 %all-to-all-start.1 = ((bf16[4,128,256]{1,2,0:T(8,128)(2,1)}), bf16[4,128,256]{1,2,0:T(8,128)(2,1)S(1)}, u32[]{:S(2)}, u32[]{:S(2)}) async-start(bf16[4,128,256]{1,2,0:T(8,128)(2,1)} %copy.36), calls=%async_computation.1 | async-start | bytes 524288 | tf_op jit(solution)/shard_map/all_to_all | solution.py:153
Sparse Core Ops, SparseCore 0:
  9.6 91.2 all-gather.2
